TPU v7x, 32 devices: a whole 2x2x4 slice. The times are simulated.
32 devices in a mesh: gx: 8 (over z, x), gy: 4 (over y, core).
Axes of the slice: x: 2, y: 2, z: 4, core: 2. Of those that a mesh axis runs over, the one named last changes fastest.
Arguments:
- inputs: bfloat16 [3, 256, 8192], P(None, 'gy', 'gx'), may hold values from -600 to 600
- norm_gain: bfloat16 [8192], P('gx'), may hold values from 0.099609375 to 1.8984375
- query_weight: bfloat16 [8192, 8192], P('gx', 'gy'), may hold values from -0.0625 to 0.0625
- key_weight: bfloat16 [8192, 1024], P('gx', 'gy'), may hold values from -0.0625 to 0.0625
- value_weight: bfloat16 [8192, 1024], P('gx', 'gy'), may hold values from -0.0625 to 0.0625
- output_weight: bfloat16 [8192, 8192], P('gy', 'gx'), may hold values from -0.0625 to 0.0625
- query_down: bfloat16 [256, 8192, 64], P('gy', 'gx'), may hold values from -0.0625 to 0.0625
- query_up: bfloat16 [256, 64, 8192], P('gx', None, 'gy'), may hold values from -0.75 to 0.75
- output_down: bfloat16 [256, 8192, 64], P('gx', 'gy'), may hold values from -0.0625 to 0.0625
- output_up: bfloat16 [256, 64, 8192], P('gy', None, 'gx'), may hold values from -0.75 to 0.75
- block_adapter: int32 [2], replicated, may hold values from 0 to 255
- cache_lengths: int32 [256], P(('gx', 'gy')), may hold values from 1 to 256, as said below
- cache_keys: bfloat16 [256, 256, 1024], P(('gx', 'gy')), may hold values from -160 to 160
- cache_values: bfloat16 [256, 256, 1024], P(('gx', 'gy')), may hold values from -6 to 6
Outputs:
- block_output: bfloat16 [3, 256, 8192], P(None, 'gy', 'gx')
Inputs may be any that keep to these rules, and one draw needn't show every extreme that they name: `cache_lengths`: some request has exactly 256 cached positions.
All inputs are finite; a program needn't handle non-finite values.
Results may differ from a plain program's by a relative error of at most 0.012.
The roundings to bfloat16 on the way count: a program that leaves them out, or rounds other values in their place, can miss the bound.
Values may be sent and summed in bfloat16 or wider, within the bound.
No kernel may reach another device: no remote copies, remote signals or barrier semaphores. Data moves between devices by JAX's collectives and lax.ppermute only.
A program may use at most 192 MiB of HBM per device.

v0:
```python
import jax
import jax.numpy as jnp
from jax import lax
from jax.sharding import PartitionSpec as P

D = 8192
QUERY_HEADS = 64
KEY_VALUE_HEADS = 8
HEAD_FEATURES = 128
BLOCK = 128
STEPS = 3
EPS = 1e-05
THETA = 500000.0


def rotary_embedding(values_in, token_positions):
    half_size = values_in.shape[-1] // 2
    exponent = jnp.arange(half_size, dtype=jnp.float32) * 2.0 / values_in.shape[-1]
    frequency = THETA ** (-exponent)
    angles = token_positions.astype(jnp.float32)[:, None] * frequency[None, :]
    cosine = jnp.cos(angles)[:, None, :]
    sine_part = jnp.sin(angles)[:, None, :]
    lower = values_in[..., :half_size]
    upper = values_in[..., half_size:]
    return jnp.concatenate(
        [lower * cosine - upper * sine_part, upper * cosine + lower * sine_part], axis=-1
    )


def pick_adapters(table, adapter_ids, first_id):
    table_count = table.shape[0]
    wanted = first_id + jnp.arange(table_count, dtype=jnp.int32)
    onehot = (adapter_ids[:, None] == wanted[None, :]).astype(table.dtype)
    flat_table = table.reshape(table_count, -1)
    picked = jnp.dot(onehot, flat_table, preferred_element_type=jnp.float32).astype(table.dtype)
    return picked.reshape((adapter_ids.shape[0],) + table.shape[1:])


def attend(
    query_rows, previous_keys, previous_values, incoming_keys, incoming_values, lengths, step_index
):
    count_of_rows = query_rows.shape[0]
    context_window = previous_keys.shape[1]
    grouped_heads = query_rows.reshape(
        count_of_rows, KEY_VALUE_HEADS, QUERY_HEADS // KEY_VALUE_HEADS, HEAD_FEATURES
    )
    keys_previous = previous_keys.reshape(
        count_of_rows, context_window, KEY_VALUE_HEADS, HEAD_FEATURES
    )
    values_previous = previous_values.reshape(
        count_of_rows, context_window, KEY_VALUE_HEADS, HEAD_FEATURES
    )
    keys_incoming = incoming_keys.reshape(count_of_rows, -1, KEY_VALUE_HEADS, HEAD_FEATURES)
    values_incoming = incoming_values.reshape(count_of_rows, -1, KEY_VALUE_HEADS, HEAD_FEATURES)
    factor = HEAD_FEATURES ** (-0.5)
    score_old = (
        jnp.einsum(
            "rhgd,rchd->rhgc", grouped_heads, keys_previous, preferred_element_type=jnp.float32
        )
        * factor
    )
    score_new = (
        jnp.einsum(
            "rhgd,rshd->rhgs", grouped_heads, keys_incoming, preferred_element_type=jnp.float32
        )
        * factor
    )
    live_old = (jnp.arange(context_window, dtype=jnp.int32)[None, :] < lengths[:, None])[
        :, None, None, :
    ]
    live_new = (jnp.arange(keys_incoming.shape[1], dtype=jnp.int32) <= step_index)[
        None, None, None, :
    ]
    score_old = jnp.where(live_old, score_old, -1e30)
    score_new = jnp.where(live_new, score_new, -1e30)
    peak_score = jnp.maximum(jnp.max(score_old, axis=-1), jnp.max(score_new, axis=-1))
    weight_old = jnp.where(live_old, jnp.exp(score_old - peak_score[..., None]), 0.0)
    weight_new = jnp.where(live_new, jnp.exp(score_new - peak_score[..., None]), 0.0)
    weight_sum = jnp.sum(weight_old, axis=-1) + jnp.sum(weight_new, axis=-1)
    mixed_out = jnp.einsum(
        "rhgc,rchd->rhgd",
        weight_old.astype(jnp.bfloat16),
        values_previous,
        preferred_element_type=jnp.float32,
    )
    mixed_out = mixed_out + jnp.einsum(
        "rhgs,rshd->rhgd",
        weight_new.astype(jnp.bfloat16),
        values_incoming,
        preferred_element_type=jnp.float32,
    )
    return (mixed_out / weight_sum[..., None]).reshape(count_of_rows, -1).astype(jnp.bfloat16)


def normalize(rows_in, squares, norm_scale):
    factor_rows = lax.rsqrt(squares / D + EPS)
    return (rows_in.astype(jnp.float32) * factor_rows[:, None] * norm_scale[None, :]).astype(
        jnp.bfloat16
    )


def local(
    inputs,
    norm_gain,
    query_weight,
    key_weight,
    value_weight,
    output_weight,
    query_down,
    query_up,
    output_down,
    output_up,
    block_adapter,
    cache_lengths,
    cache_keys,
    cache_values,
):
    across_second = lax.axis_size("gy")
    index_first = lax.axis_index("gx")
    index_second = lax.axis_index("gy")
    request_count = inputs.shape[1] * across_second
    local_rows = cache_keys.shape[0]
    block_count = block_adapter.shape[0]
    norm_scale = norm_gain.astype(jnp.float32)
    query_first = pick_adapters(query_down, block_adapter, index_second * query_down.shape[0])
    query_second = pick_adapters(query_up, block_adapter, index_first * query_up.shape[0])
    output_first = pick_adapters(output_down, block_adapter, index_first * output_down.shape[0])
    output_second = pick_adapters(output_up, block_adapter, index_second * output_up.shape[0])
    incoming_keys = jnp.zeros((local_rows, STEPS, cache_keys.shape[2]), jnp.bfloat16)
    incoming_values = jnp.zeros((local_rows, STEPS, cache_values.shape[2]), jnp.bfloat16)
    results = []
    for step_index in range(STEPS):
        own_inputs = inputs[step_index]
        rows_all = lax.all_gather(own_inputs, "gy", axis=0, tiled=True)
        squares = lax.psum(jnp.sum(jnp.square(rows_all.astype(jnp.float32)), axis=1), "gx")
        normed = normalize(rows_all, squares, norm_scale)
        blocked = normed.reshape(block_count, BLOCK, -1)
        rank_part = jnp.einsum(
            "bnd,bdr->bnr", blocked, query_first, preferred_element_type=jnp.float32
        )
        rank_query = lax.psum(rank_part, ("gx", "gy")).astype(jnp.bfloat16)
        delta_query = jnp.einsum(
            "bnr,bre->bne", rank_query, query_second, preferred_element_type=jnp.float32
        ).reshape(request_count, -1)
        part_query = jnp.dot(normed, query_weight, preferred_element_type=jnp.float32) + delta_query
        part_key = jnp.dot(normed, key_weight, preferred_element_type=jnp.float32)
        part_value = jnp.dot(normed, value_weight, preferred_element_type=jnp.float32)
        summed = (
            lax.psum_scatter(part_query, "gx", scatter_dimension=0, tiled=True),
            lax.psum_scatter(part_key, "gx", scatter_dimension=0, tiled=True),
            lax.psum_scatter(part_value, "gx", scatter_dimension=0, tiled=True),
        )
        query_full, key_complete, value_full = (
            lax.all_to_all(
                summed[0].astype(jnp.bfloat16), "gy", split_axis=0, concat_axis=1, tiled=True
            ),
            lax.all_to_all(
                summed[1].astype(jnp.bfloat16), "gy", split_axis=0, concat_axis=1, tiled=True
            ),
            lax.all_to_all(
                summed[2].astype(jnp.bfloat16), "gy", split_axis=0, concat_axis=1, tiled=True
            ),
        )
        token_positions = cache_lengths + step_index
        query_rot = rotary_embedding(
            query_full.astype(jnp.float32).reshape(local_rows, QUERY_HEADS, HEAD_FEATURES),
            token_positions,
        ).astype(jnp.bfloat16)
        key_rotated = rotary_embedding(
            key_complete.astype(jnp.float32).reshape(local_rows, KEY_VALUE_HEADS, HEAD_FEATURES),
            token_positions,
        ).astype(jnp.bfloat16)
        incoming_keys = incoming_keys.at[:, step_index].set(key_rotated.reshape(local_rows, -1))
        incoming_values = incoming_values.at[:, step_index].set(value_full)
        mixed_local = attend(
            query_rot.reshape(local_rows, -1),
            cache_keys,
            cache_values,
            incoming_keys,
            incoming_values,
            cache_lengths,
            step_index,
        )
        head_group = lax.all_to_all(mixed_local, "gy", split_axis=1, concat_axis=0, tiled=True)
        mixed_all = lax.all_gather(head_group, "gx", axis=0, tiled=True)
        rank_part_out = jnp.einsum(
            "bnq,bqr->bnr",
            mixed_all.reshape(block_count, BLOCK, -1),
            output_first,
            preferred_element_type=jnp.float32,
        )
        rank_output = lax.psum(rank_part_out, ("gx", "gy")).astype(jnp.bfloat16)
        delta_output = jnp.einsum(
            "bnr,bre->bne", rank_output, output_second, preferred_element_type=jnp.float32
        ).reshape(request_count, -1)
        partial_out = (
            jnp.dot(mixed_all, output_weight, preferred_element_type=jnp.float32) + delta_output
        )
        results.append(
            lax.psum_scatter(partial_out, "gy", scatter_dimension=0, tiled=True).astype(
                jnp.bfloat16
            )
        )
    return jnp.stack(results)


def solution(mesh):
    in_specs = (
        P(None, "gy", "gx"),
        P("gx"),
        P("gx", "gy"),
        P("gx", "gy"),
        P("gx", "gy"),
        P("gy", "gx"),
        P("gy", "gx", None),
        P("gx", None, "gy"),
        P("gx", "gy", None),
        P("gy", None, "gx"),
        P(),
        P(("gx", "gy")),
        P(("gx", "gy"), None, None),
        P(("gx", "gy"), None, None),
    )
    out_specs = P(None, "gy", "gx")
    return jax.shard_map(local, mesh=mesh, in_specs=in_specs, out_specs=out_specs, check_vma=False)
```

profile of v0, /device:TPU:0, one launch (start us, length us, event | category | flops | bytes accessed | tf_op | source)
XLA Modules:
  0.0 941.0 jit_solution(17731421883246101163)
XLA Ops:
  7.7 8.6 all-gather.2
  16.3 7.3 all-gather
  23.8 7.3 all-gather.1
  32.3 21.7 %all-reduce.4 = (f32[256]{0:T(256)S(1)}, f32[256]{0:T(256)S(1)}, f32[256]{0:T(256)S(1)}) all-reduce(f32[256]{0:T(256)S(1)} %fusion.66, f32[256]{0:T(256)S(1)} %fusion.69, f32[256]{0:T(256)S(1)} %fusion.72), channel_id=1, replica_groups=mesh['gx'=8,'gy'=4] {'gx'}, use_global_device_ids=true, to_apply=%region_1.0 | all-reduce | flops 768 | bytes 6144 | tf_op jit(solution)/shard_map/psum | solution.py:135
  57.6 2.1 fusion.185
  59.7 2.1 fusion.189
  64.5 11.4 %copy.109 = bf16[4,8,64,2048]{3,1,2,0:T(8,128)(2,1)} copy(bf16[4,8,64,2048]{3,2,1,0:T(8,128)(2,1)} %bitcast.289) | data formatting | bytes 16777216
  75.9 15.6 %copy.74 = bf16[64,1024,64]{2,1,0:T(8,128)(2,1)} copy(bf16[64,1024,64]{1,2,0:T(8,128)(2,1)} %param.32) | data formatting | bytes 16777216 | tf_op args[6]
  91.5 16.5 %reshape.597 = bf16[64,65536]{1,0:T(8,128)(2,1)} reshape(bf16[64,1024,64]{2,1,0:T(8,128)(2,1)} %copy.74) | data formatting | bytes 16777216 | tf_op jit(solution)/shard_map/reshape | solution.py:34
  108.0 4.7 convolution_convert_fusion.3
  114.1 4.7 convolution_convert_fusion.1
  118.7 40.4 %all-reduce.7 = (bf16[2,128,64]{1,2,0:T(8,128)(2,1)S(1)}, bf16[2,128,64]{1,2,0:T(8,128)(2,1)S(1)}, bf16[2,128,64]{1,2,0:T(8,128)(2,1)S(1)}) all-reduce(f32[2,128,64]{1,2,0:T(8,128)S(1)} %fusion.191, f32[2,128,64]{1,2,0:T(8,128)S(1)} %fusion.183, f32[2,128,64]{1,2,0:T(8,128)S(1)} %fusion.187), channel_id=1, replica_groups=mesh['gx'=8,'gy'=4] {'gx','gy'}, use_global_device_ids=true, to_apply=%region_26.27 | all-reduce | flops 49152 | bytes 294912 | tf_op jit(solution)/shard_map/psum | solution.py:141
  159.7 4.8 convolution_add_fusion.1
  165.1 4.9 convolution_add_fusion
  170.5 4.8 convolution_add_fusion.2
  177.0 3.3 all-to-all-start.1
  181.6 60.8 %reduce-scatter.17.cloned.1.call-done = f32[32,256]{1,0:T(8,128)} async-done(((f32[256,256]{1,0:T(8,128)}), f32[32,256]{1,0:T(8,128)}) %reduce-scatter.17.cloned.1.call-update) | async-done | bytes 32784 | tf_op jit(solution)/shard_map/reduce_scatter | solution.py:151
  243.9 62.1 %reduce-scatter.25.cloned.1.call-done = f32[32,256]{1,0:T(8,128)} async-done(((f32[256,256]{1,0:T(8,128)}), f32[32,256]{1,0:T(8,128)}) %reduce-scatter.25.cloned.1.call-update) | async-done | bytes 32784 | tf_op jit(solution)/shard_map/reduce_scatter | solution.py:151
  307.3 62.1 %reduce-scatter.31.cloned.1.call-done = f32[32,256]{1,0:T(8,128)} async-done(((f32[256,256]{1,0:T(8,128)}), f32[32,256]{1,0:T(8,128)}) %reduce-scatter.31.cloned.1.call-update) | async-done | bytes 32784 | tf_op jit(solution)/shard_map/reduce_scatter | solution.py:150
  370.8 62.2 %reduce-scatter.33.cloned.1.call-done = f32[32,256]{1,0:T(8,128)} async-done(((f32[256,256]{1,0:T(8,128)}), f32[32,256]{1,0:T(8,128)}) %reduce-scatter.33.cloned.1.call-update) | async-done | bytes 32784 | tf_op jit(solution)/shard_map/reduce_scatter | solution.py:151
  434.3 3.2 all-to-all-start.5
  437.8 3.6 all-to-all-done.5
  441.4 3.2 all-to-all-start.9
  444.8 3.7 all-to-all-done.9
  448.5 3.2 all-to-all-start.2
  451.8 3.7 all-to-all-done.2
  455.6 3.2 all-to-all-start.6
  459.0 3.6 all-to-all-done.6
  462.6 40.5 %reduce-scatter.21.cloned.1.call-done = f32[32,2048]{1,0:T(8,128)} async-done(((f32[256,2048]{1,0:T(8,128)}), f32[32,2048]{1,0:T(8,128)}) %reduce-scatter.21.cloned.1.call-update) | async-done | bytes 262160 | tf_op jit(solution)/shard_map/reduce_scatter | solution.py:149
  503.2 1.6 convert_bitcast_fusion.6
  504.8 3.3 all-to-all-start.4
  508.1 65.3 %reduce-scatter.29.cloned.1.call-done = f32[32,2048]{1,0:T(8,128)} async-done(((f32[256,2048]{1,0:T(8,128)}), f32[32,2048]{1,0:T(8,128)}) %reduce-scatter.29.cloned.1.call-update) | async-done | bytes 262160 | tf_op jit(solution)/shard_map/reduce_scatter | solution.py:149
  573.4 1.6 convert_bitcast_fusion.4
  575.0 68.6 %reduce-scatter.13.cloned.1.call-done = f32[32,2048]{1,0:T(8,128)} async-done(((f32[256,2048]{1,0:T(8,128)}), f32[32,2048]{1,0:T(8,128)}) %reduce-scatter.13.cloned.1.call-update) | async-done | bytes 262160 | tf_op jit(solution)/shard_map/reduce_scatter | solution.py:149
  643.6 1.6 convert_bitcast_fusion.8
  645.3 3.3 all-to-all-start.8
  649.1 4.1 all-to-all-done.8
  653.2 3.2 all-to-all-start.10
  657.3 3.7 fusion.181
  663.1 3.3 all-to-all-start
  667.2 3.8 all-to-all-done
  671.5 3.6 fusion.179
  677.0 7.7 all_to_all.174
  684.9 2.9 fusion.57
  688.0 7.7 all_to_all.175
  696.3 2.9 fusion.63
  699.3 7.7 all_to_all.176
  707.1 12.0 %copy.113 = bf16[8,8,64,1024]{3,1,2,0:T(8,128)(2,1)} copy(bf16[8,8,64,1024]{3,2,1,0:T(8,128)(2,1)} %bitcast.290) | data formatting | bytes 16777216
  719.1 15.8 %copy.83 = bf16[32,2048,64]{2,1,0:T(8,128)(2,1)} copy(bf16[32,2048,64]{1,2,0:T(8,128)(2,1)} %param.34) | data formatting | bytes 16777216 | tf_op args[8]
  734.9 15.9 %reshape.608 = bf16[32,131072]{1,0:T(8,128)(2,1)} reshape(bf16[32,2048,64]{2,1,0:T(8,128)(2,1)} %copy.83) | data formatting | bytes 16777216 | tf_op jit(solution)/shard_map/reshape | solution.py:34
  750.8 4.7 convolution_convert_fusion
  756.2 4.7 convolution_convert_fusion.2
  760.9 1.9 fusion.194
  762.7 1.5 all-gather.9.cloned.1.call-done
  764.2 1.7 fusion.190
  765.9 39.2 %all-gather.7.cloned.1.call-done = bf16[256,2048]{1,0:T(8,128)(2,1)} async-done(((bf16[32,2048]{1,0:T(8,128)(2,1)}), bf16[256,2048]{1,0:T(8,128)(2,1)}) %all-gather.7.cloned.1.call-update) | async-done | bytes 1048592 | tf_op jit(solution)/shard_map/all_gather | solution.py:185
  805.1 1.7 fusion.186
  806.9 41.8 %all-reduce.8 = (bf16[2,128,64]{1,2,0:T(8,128)(2,1)S(1)}, bf16[2,128,64]{1,2,0:T(8,128)(2,1)S(1)}, bf16[2,128,64]{1,2,0:T(8,128)(2,1)S(1)}) all-reduce(f32[2,128,64]{1,2,0:T(8,128)S(1)} %fusion.194, f32[2,128,64]{1,2,0:T(8,128)S(1)} %fusion.190, f32[2,128,64]{1,2,0:T(8,128)S(1)} %fusion.186), channel_id=1, replica_groups=mesh['gx'=8,'gy'=4] {'gx','gy'}, use_global_device_ids=true, to_apply=%region_34.35 | all-reduce | flops 49152 | bytes 294912 | tf_op jit(solution)/shard_map/psum | solution.py:192
  849.1 4.5 convolution_add_fusion.3
  854.0 4.6 convolution_add_fusion.4
  859.0 4.7 convolution_add_fusion.5
  863.8 13.7 %reduce-scatter.35.cloned.1.call-done = f32[64,1024]{1,0:T(8,128)} async-done(((f32[256,1024]{1,0:T(8,128)}), f32[64,1024]{1,0:T(8,128)}) %reduce-scatter.35.cloned.1.call-update) | async-done | bytes 262160 | tf_op jit(solution)/shard_map/reduce_scatter | solution.py:200
  878.4 26.5 %reduce-scatter.27.cloned.1.call-done = f32[64,1024]{1,0:T(8,128)} async-done(((f32[256,1024]{1,0:T(8,128)}), f32[64,1024]{1,0:T(8,128)}) %reduce-scatter.27.cloned.1.call-update) | async-done | bytes 262160 | tf_op jit(solution)/shard_map/reduce_scatter | solution.py:200
  905.9 26.4 %reduce-scatter.19.cloned.1.call-done = f32[64,1024]{1,0:T(8,128)} async-done(((f32[256,1024]{1,0:T(8,128)}), f32[64,1024]{1,0:T(8,128)}) %reduce-scatter.19.cloned.1.call-update) | async-done | bytes 262160 | tf_op jit(solution)/shard_map/reduce_scatter | solution.py:200
  (158 shorter events, 33.7 us)
Async XLA Ops:
  6.5 48.9 %copy-start = (bf16[1024,256]{1,0:T(8,128)(2,1)S(1)}, bf16[1024,256]{1,0:T(8,128)(2,1)}, u32[]{:S(2)}) copy-start(bf16[1024,256]{1,0:T(8,128)(2,1)} %param.29) | copy-start | bytes 1572868
  6.5 25.7 %copy-start.9 = (bf16[1024]{0:T(1024)(128)(2,1)S(1)}, bf16[1024]{0:T(1024)(128)(2,1)}, u32[]{:S(2)}) copy-start(bf16[1024]{0:T(1024)(128)(2,1)} %param.27) | copy-start | bytes 6148
  6.5 169.1 %reduce-scatter.15.cloned.1.call-start = ((), (), s32[]{:S(2)}) async-start(), calls=%async_computation.25 | async-start | bytes 294912 | tf_op jit(solution)/shard_map/reduce_scatter | solution.py:150
  31.1 0.8 copy-start.3
  55.4 7.5 copy-start.4
  56.5 123.8 %reduce-scatter.23.cloned.1.call-start = ((), (), s32[]{:S(2)}) async-start(), calls=%async_computation.30 | async-start | bytes 294912 | tf_op jit(solution)/shard_map/reduce_scatter | solution.py:150
  57.5 185.0 %reduce-scatter.17.cloned.1.call-start = ((), (), s32[]{:S(2)}) async-start(), calls=%async_computation.26 | async-start | bytes 294912 | tf_op jit(solution)/shard_map/reduce_scatter | solution.py:151
  59.7 246.3 %reduce-scatter.25.cloned.1.call-start = ((), (), s32[]{:S(2)}) async-start(), calls=%async_computation.31 | async-start | bytes 294912 | tf_op jit(solution)/shard_map/reduce_scatter | solution.py:151
  61.8 307.7 %reduce-scatter.31.cloned.1.call-start = ((), (), s32[]{:S(2)}) async-start(), calls=%async_computation.35 | async-start | bytes 294912 | tf_op jit(solution)/shard_map/reduce_scatter | solution.py:150
  62.9 370.1 %reduce-scatter.33.cloned.1.call-start = ((), (), s32[]{:S(2)}) async-start(), calls=%async_computation.36 | async-start | bytes 294912 | tf_op jit(solution)/shard_map/reduce_scatter | solution.py:151
  63.9 439.2 %reduce-scatter.21.cloned.1.call-start = ((), (), s32[]{:S(2)}) async-start(), calls=%async_computation.29 | async-start | bytes 2359296 | tf_op jit(solution)/shard_map/reduce_scatter | solution.py:149
  91.5 16.5 %copy-start.8 = (s32[2]{0:T(128)S(1)}, s32[2]{0:T(128)}, u32[]{:S(2)}) copy-start(s32[2]{0:T(128)} %param.36) | copy-start | bytes 28
  164.5 408.9 %reduce-scatter.29.cloned.1.call-start = ((), (), s32[]{:S(2)}) async-start(), calls=%async_computation.34 | async-start | bytes 2359296 | tf_op jit(solution)/shard_map/reduce_scatter | solution.py:149
  169.9 473.7 %reduce-scatter.13.cloned.1.call-start = ((), (), s32[]{:S(2)}) async-start(), calls=%async_computation.24 | async-start | bytes 2359296 | tf_op jit(solution)/shard_map/reduce_scatter | solution.py:149
  170.5 4.9 copy-start.10
  177.0 257.3 %all-to-all-start.1 = ((bf16[4,8,256]{2,1,0:T(8,128)(2,1)}), bf16[4,8,256]{2,1,0:T(8,128)(2,1)S(1)}, u32[]{:S(2)}, u32[]{:S(2)}) async-start(bf16[4,8,256]{2,1,0:T(8,128)(2,1)} %convert_bitcast_fusion.15), calls=%async_computation.3 | async-start | bytes 32768 | tf_op jit(solution)/shard_map/all_to_all | solution.py:157
  434.3 7.1 all-to-all-start.5
  441.4 7.1 all-to-all-start.9
  448.5 7.1 all-to-all-start.2
  455.6 7.1 all-to-all-start.6
  504.8 140.5 %all-to-all-start.4 = ((bf16[4,8,2048]{2,1,0:T(8,128)(2,1)}), bf16[4,8,2048]{2,1,0:T(8,128)(2,1)S(1)}, u32[]{:S(2)}, u32[]{:S(2)}) async-start(bf16[4,8,2048]{2,1,0:T(8,128)(2,1)} %convert_bitcast_fusion.6), calls=%async_computation.9 | async-start | bytes 262144 | tf_op jit(solution)/shard_map/all_to_all | solution.py:154
  645.3 7.9 all-to-all-start.8
  653.2 9.9 %all-to-all-start.10 = ((bf16[4,8,256]{2,1,0:T(8,128)(2,1)}), bf16[4,8,256]{2,1,0:T(8,128)(2,1)S(1)}, u32[]{:S(2)}, u32[]{:S(2)}) async-start(bf16[4,8,256]{2,1,0:T(8,128)(2,1)} %convert_bitcast_fusion.10), calls=%async_computation.21 | async-start | bytes 32768 | tf_op jit(solution)/shard_map/all_to_all | solution.py:160
  656.8 4.3 copy-start.2
  663.1 7.9 all-to-all-start
  666.4 94.4 %all-gather.11.cloned.1.call-start = ((), (), s32[]{:S(2)}) async-start(), calls=%async_computation.37 | async-start | bytes 1179648 | tf_op jit(solution)/shard_map/all_gather | solution.py:185
  671.4 4.8 copy-start.11
  684.7 79.5 %all-gather.9.cloned.1.call-start = ((), (), s32[]{:S(2)}) async-start(), calls=%async_computation.32 | async-start | bytes 1179648 | tf_op jit(solution)/shard_map/all_gather | solution.py:185
  695.7 109.4 %all-gather.7.cloned.1.call-start = ((), (), s32[]{:S(2)}) async-start(), calls=%async_computation.27 | async-start | bytes 1179648 | tf_op jit(solution)/shard_map/all_gather | solution.py:185
  707.0 170.4 %reduce-scatter.35.cloned.1.call-start = ((), (), s32[]{:S(2)}) async-start(), calls=%async_computation.38 | async-start | bytes 1310720 | tf_op jit(solution)/shard_map/reduce_scatter | solution.py:200
  760.9 88.2 %copy-start.5 = (bf16[256,2048]{1,0:T(8,128)(2,1)S(1)}, bf16[256,2048]{1,0:T(8,128)(2,1)}, u32[]{:S(2)}) copy-start(bf16[256,2048]{1,0:T(8,128)(2,1)} %all-gather.11.cloned.1.call-done) | copy-start | bytes 3145732
  849.0 4.9 copy-start.6
  853.6 51.4 %reduce-scatter.27.cloned.1.call-start = ((), (), s32[]{:S(2)}) async-start(), calls=%async_computation.33 | async-start | bytes 1310720 | tf_op jit(solution)/shard_map/reduce_scatter | solution.py:200
  854.0 5.0 copy-start.7
  858.6 73.7 %reduce-scatter.19.cloned.1.call-start = ((), (), s32[]{:S(2)}) async-start(), calls=%async_computation.28 | async-start | bytes 1310720 | tf_op jit(solution)/shard_map/reduce_scatter | solution.py:200
  859.0 75.0 %copy-start.1 = (bf16[1024,256]{1,0:T(8,128)(2,1)S(1)}, bf16[1024,256]{1,0:T(8,128)(2,1)}, u32[]{:S(2)}) copy-start(bf16[1024,256]{1,0:T(8,128)(2,1)} %param.29) | copy-start | bytes 1572868
Sparse Core Ops, SparseCore 0:
  56.6 58.5 reduce-scatter.14
  118.5 60.3 reduce-scatter.22
  182.2 60.2 reduce-scatter.16
  245.7 60.2 reduce-scatter.24
  309.2 60.2 reduce-scatter.30
  372.6 60.2 reduce-scatter.32
  436.5 66.6 reduce-scatter.20
  506.7 66.6 reduce-scatter.28
  576.9 66.6 reduce-scatter.12
  684.8 38.2 all-gather.10
  725.3 38.8 all-gather.8
  766.2 38.8 all-gather.6
  853.7 23.7 reduce-scatter.34
  880.0 24.8 reduce-scatter.26
  907.3 24.9 reduce-scatter.18
where the time goes:
time: 947 us; the launch traced here: 941 us
  waiting for transfers between devices  552 us (58%)
  blocking collectives  150 us (16%)
  local copies, waits for them, and re-layouts  91.7 us (10%)
  matrix products  81.2 us (9%)
  starting transfers between devices  30.7 us (3%)
  other arithmetic  21.1 us (2%)
  between operations  14.5 us (2%)
    reduce_scatter x3, waiting for transfers between devices, local(): lax.psum_scatter(part_value, 'gx', scatter_dimension=0, tiled=True)  185 us
    reduce_scatter x3, waiting for transfers between devices, local(): lax.psum_scatter(part_query, 'gx', scatter_dimension=0, tiled=True)  174 us
    reduce_scatter x3, waiting for transfers between devices, local(): lax.psum_scatter(partial_out, 'gy', scatter_dimension=0, tiled=True)  66.6 us
    reduce_scatter x3, waiting for transfers between devices, local(): lax.psum_scatter(part_key, 'gx', scatter_dimension=0, tiled=True)  62.2 us
    unnamed x34, local copies, waits for them, and re-layouts  55.8 us
    psum x1, blocking collectives, local(): rank_output = lax.psum(rank_part_out, ('gx', 'gy')).astype(jnp.bfloat16)  41.8 us
    all_gather x3, waiting for transfers between devices, local(): mixed_all = lax.all_gather(head_group, 'gx', axis=0, tiled=True)  40.7 us
    psum x1, blocking collectives, local(): rank_query = lax.psum(rank_part, ('gx', 'gy')).astype(jnp.bfloat16)  40.4 us
  transfers between devices with their start and end apart: 24, of which 18 were waited for; matrix products, arithmetic and copies ran while one was open for 19% of the time, Pallas kernels for 0%

commit v1 on v0

--- a/solution.py
+++ b/solution.py
@@ -182,7 +182,18 @@
             step_index,
         )
         head_group = lax.all_to_all(mixed_local, "gy", split_axis=1, concat_axis=0, tiled=True)
-        mixed_all = lax.all_gather(head_group, "gx", axis=0, tiled=True)
+        peers, position, rows = (lax.axis_size("gx"), lax.axis_index("gx"), head_group.shape[0])
+        ahead = [(i, (i + 1) % peers) for i in range(peers)]
+        filled = jnp.zeros(
+            (*head_group.shape[:0], peers * rows, *head_group.shape[0 + 1 :]), head_group.dtype
+        )
+        held = head_group
+        for lap in range(peers):
+            owner = (position - lap) % peers
+            filled = lax.dynamic_update_slice_in_dim(filled, held, owner * rows, axis=0)
+            if lap < peers - 1:
+                held = lax.ppermute(held, "gx", ahead)
+        mixed_all = filled
         rank_part_out = jnp.einsum(
             "bnq,bqr->bnr",
             mixed_all.reshape(block_count, BLOCK, -1),

time: 947 us -> 912 us (0.963)
  waiting for transfers between devices: 552 us -> 526 us
  blocking collectives: 150 us -> 126 us
  starting transfers between devices: 30.7 us -> 44.9 us
    ppermute x0 -> x21, waiting for transfers between devices: none -> 61.1 us  [local(): held = lax.ppermute(held, 'gx', ahead)]
    reduce_scatter x3, waiting for transfers between devices: 185 us -> 137 us  [local(): lax.psum_scatter(part_value, 'gx', scatter_dimension=0, tiled=True)]
    all_gather x3 -> x0, waiting for transfers between devices: 40.7 us -> none  [local(): mixed_all = lax.all_gather(head_group, 'gx', axis=0, tiled=True)]
    all_to_all x3 -> x0, blocking collectives: 23.1 us -> none  [local(): lax.all_to_all(mixed_local, 'gy', split_axis=1, concat_axis=0, tiled=True)]
    all_to_all x0 -> x3, starting transfers between devices: none -> 9.97 us  [local(): lax.all_to_all(mixed_local, 'gy', split_axis=1, concat_axis=0, tiled=True)]
  transfers between devices with their start and end apart: 24 -> 45, of which waited for: 18 -> 39; matrix products, arithmetic and copies ran while one was open for 19% -> 19% of each run, Pallas kernels for 0% -> 0%
where the time goes in v1:
time: 912 us; the launch traced here: 905 us
  waiting for transfers between devices  526 us (58%)
  blocking collectives  126 us (14%)
  local copies, waits for them, and re-layouts  94.4 us (10%)
  matrix products  77.7 us (9%)
  starting transfers between devices  44.9 us (5%)
  other arithmetic  21.1 us (2%)
  between operations  14.9 us (2%)
    reduce_scatter x3, waiting for transfers between devices, local(): lax.psum_scatter(part_query, 'gx', scatter_dimension=0, tiled=True)  174 us
    reduce_scatter x3, waiting for transfers between devices, local(): lax.psum_scatter(part_value, 'gx', scatter_dimension=0, tiled=True)  137 us
    reduce_scatter x3, waiting for transfers between devices, local(): lax.psum_scatter(partial_out, 'gy', scatter_dimension=0, tiled=True)  67.7 us
    reduce_scatter x3, waiting for transfers between devices, local(): lax.psum_scatter(part_key, 'gx', scatter_dimension=0, tiled=True)  62.2 us
    ppermute x21, waiting for transfers between devices, local(): held = lax.ppermute(held, 'gx', ahead)  61.1 us
    unnamed x34, local copies, waits for them, and re-layouts  55.7 us
    psum x1, blocking collectives, local(): rank_output = lax.psum(rank_part_out, ('gx', 'gy')).astype(jnp.bfloat16)  41.1 us
    psum x1, blocking collectives, local(): rank_query = lax.psum(rank_part, ('gx', 'gy')).astype(jnp.bfloat16)  40.4 us
  transfers between devices with their start and end apart: 45, of which 39 were waited for; matrix products, arithmetic and copies ran while one was open for 19% of the time, Pallas kernels for 0%

profile of v1, /device:TPU:0, one launch (start us, length us, event | category | flops | bytes accessed | tf_op | source)
XLA Modules:
  0.0 905.3 jit_solution(11279937535175998975)
XLA Ops:
  7.7 8.6 all-gather.2
  16.3 7.3 all-gather
  23.8 7.3 all-gather.1
  32.2 21.7 %all-reduce.4 = (f32[256]{0:T(256)S(1)}, f32[256]{0:T(256)S(1)}, f32[256]{0:T(256)S(1)}) all-reduce(f32[256]{0:T(256)S(1)} %fusion.66, f32[256]{0:T(256)S(1)} %fusion.69, f32[256]{0:T(256)S(1)} %fusion.72), channel_id=1, replica_groups=mesh['gx'=8,'gy'=4] {'gx'}, use_global_device_ids=true, to_apply=%region_1.0 | all-reduce | flops 768 | bytes 6144 | tf_op jit(solution)/shard_map/psum | solution.py:135
  64.6 11.5 %copy.109 = bf16[4,8,64,2048]{3,1,2,0:T(8,128)(2,1)} copy(bf16[4,8,64,2048]{3,2,1,0:T(8,128)(2,1)} %bitcast.292) | data formatting | bytes 16777216
  76.0 15.6 %copy.74 = bf16[64,1024,64]{2,1,0:T(8,128)(2,1)} copy(bf16[64,1024,64]{1,2,0:T(8,128)(2,1)} %param.32) | data formatting | bytes 16777216 | tf_op args[6]
  91.7 16.6 %reshape.597 = bf16[64,65536]{1,0:T(8,128)(2,1)} reshape(bf16[64,1024,64]{2,1,0:T(8,128)(2,1)} %copy.74) | data formatting | bytes 16777216 | tf_op jit(solution)/shard_map/reshape | solution.py:34
  108.3 4.7 convolution_convert_fusion.3
  114.3 4.7 convolution_convert_fusion.1
  118.9 40.4 %all-reduce.7 = (bf16[2,128,64]{1,2,0:T(8,128)(2,1)S(1)}, bf16[2,128,64]{1,2,0:T(8,128)(2,1)S(1)}, bf16[2,128,64]{1,2,0:T(8,128)(2,1)S(1)}) all-reduce(f32[2,128,64]{1,2,0:T(8,128)S(1)} %fusion.191, f32[2,128,64]{1,2,0:T(8,128)S(1)} %fusion.183, f32[2,128,64]{1,2,0:T(8,128)S(1)} %fusion.187), channel_id=1, replica_groups=mesh['gx'=8,'gy'=4] {'gx','gy'}, use_global_device_ids=true, to_apply=%region_26.27 | all-reduce | flops 49152 | bytes 294912 | tf_op jit(solution)/shard_map/psum | solution.py:141
  159.9 4.8 convolution_add_fusion.1
  165.2 4.9 convolution_add_fusion
  170.7 4.9 convolution_add_fusion.2
  175.8 12.0 %copy.113 = bf16[8,8,64,1024]{3,1,2,0:T(8,128)(2,1)} copy(bf16[8,8,64,1024]{3,2,1,0:T(8,128)(2,1)} %bitcast.293) | data formatting | bytes 16777216
  187.7 4.7 convolution_convert_fusion.2
  192.4 15.6 %copy.83 = bf16[32,2048,64]{2,1,0:T(8,128)(2,1)} copy(bf16[32,2048,64]{1,2,0:T(8,128)(2,1)} %param.34) | data formatting | bytes 16777216 | tf_op args[8]
  208.0 16.0 %reshape.608 = bf16[32,131072]{1,0:T(8,128)(2,1)} reshape(bf16[32,2048,64]{2,1,0:T(8,128)(2,1)} %copy.83) | data formatting | bytes 16777216 | tf_op jit(solution)/shard_map/reshape | solution.py:34
  225.6 3.3 all-to-all-start.1
  230.3 12.3 %reduce-scatter.17.cloned.1.call-done = f32[32,256]{1,0:T(8,128)} async-done(((f32[256,256]{1,0:T(8,128)}), f32[32,256]{1,0:T(8,128)}) %reduce-scatter.17.cloned.1.call-update) | async-done | bytes 32784 | tf_op jit(solution)/shard_map/reduce_scatter | solution.py:151
  243.9 62.2 %reduce-scatter.25.cloned.1.call-done = f32[32,256]{1,0:T(8,128)} async-done(((f32[256,256]{1,0:T(8,128)}), f32[32,256]{1,0:T(8,128)}) %reduce-scatter.25.cloned.1.call-update) | async-done | bytes 32784 | tf_op jit(solution)/shard_map/reduce_scatter | solution.py:151
  307.5 62.1 %reduce-scatter.31.cloned.1.call-done = f32[32,256]{1,0:T(8,128)} async-done(((f32[256,256]{1,0:T(8,128)}), f32[32,256]{1,0:T(8,128)}) %reduce-scatter.31.cloned.1.call-update) | async-done | bytes 32784 | tf_op jit(solution)/shard_map/reduce_scatter | solution.py:150
  371.0 62.2 %reduce-scatter.33.cloned.1.call-done = f32[32,256]{1,0:T(8,128)} async-done(((f32[256,256]{1,0:T(8,128)}), f32[32,256]{1,0:T(8,128)}) %reduce-scatter.33.cloned.1.call-update) | async-done | bytes 32784 | tf_op jit(solution)/shard_map/reduce_scatter | solution.py:151
  434.5 3.2 all-to-all-start.5
  438.0 3.6 all-to-all-done.5
  441.6 3.2 all-to-all-start.9
  444.9 3.7 all-to-all-done.9
  448.6 3.7 all-to-all-start.2
  452.4 3.7 all-to-all-done.2
  456.1 3.2 all-to-all-start.6
  459.6 3.6 all-to-all-done.6
  463.2 40.4 %reduce-scatter.21.cloned.1.call-done = f32[32,2048]{1,0:T(8,128)} async-done(((f32[256,2048]{1,0:T(8,128)}), f32[32,2048]{1,0:T(8,128)}) %reduce-scatter.21.cloned.1.call-update) | async-done | bytes 262160 | tf_op jit(solution)/shard_map/reduce_scatter | solution.py:149
  505.2 3.3 all-to-all-start.4
  508.5 65.2 %reduce-scatter.29.cloned.1.call-done = f32[32,2048]{1,0:T(8,128)} async-done(((f32[256,2048]{1,0:T(8,128)}), f32[32,2048]{1,0:T(8,128)}) %reduce-scatter.29.cloned.1.call-update) | async-done | bytes 262160 | tf_op jit(solution)/shard_map/reduce_scatter | solution.py:149
  575.4 68.6 %reduce-scatter.13.cloned.1.call-done = f32[32,2048]{1,0:T(8,128)} async-done(((f32[256,2048]{1,0:T(8,128)}), f32[32,2048]{1,0:T(8,128)}) %reduce-scatter.13.cloned.1.call-update) | async-done | bytes 262160 | tf_op jit(solution)/shard_map/reduce_scatter | solution.py:149
  645.6 3.3 all-to-all-start.8
  649.5 4.1 all-to-all-done.8
  653.5 3.2 all-to-all-start.10
  657.6 3.7 fusion.181
  663.4 3.3 all-to-all-start
  667.5 3.9 all-to-all-done
  671.9 3.6 fusion.179
  678.0 3.3 all-to-all-start.11
  681.4 2.9 fusion.57
  685.9 3.3 all-to-all-start.7
  689.3 2.9 fusion.63
  693.9 3.3 all-to-all-start.3
  697.3 4.6 convolution_convert_fusion
  707.3 4.7 collective-permute-done.14
  717.6 3.0 collective-permute-done.15
  723.5 3.3 collective-permute-done.1
  726.8 3.0 collective-permute-done.16
  732.5 3.0 collective-permute-done.2
  738.4 3.1 collective-permute-done.10
  741.6 3.0 collective-permute-done.3
  747.4 3.2 collective-permute-done.11
  753.5 3.0 collective-permute-done.19
  756.5 3.2 collective-permute-done.12
  770.5 41.1 %all-reduce.8 = (bf16[2,128,64]{1,2,0:T(8,128)(2,1)S(1)}, bf16[2,128,64]{1,2,0:T(8,128)(2,1)S(1)}, bf16[2,128,64]{1,2,0:T(8,128)(2,1)S(1)}) all-reduce(f32[2,128,64]{1,2,0:T(8,128)S(1)} %fusion.194, f32[2,128,64]{1,2,0:T(8,128)S(1)} %fusion.190, f32[2,128,64]{1,2,0:T(8,128)S(1)} %fusion.186), channel_id=1, replica_groups=mesh['gx'=8,'gy'=4] {'gx','gy'}, use_global_device_ids=true, to_apply=%region_34.35 | all-reduce | flops 49152 | bytes 294912 | tf_op jit(solution)/shard_map/psum | solution.py:203
  812.0 4.9 convolution_add_fusion.3
  817.3 4.4 convolution_add_fusion.4
  822.2 4.7 convolution_add_fusion.5
  826.9 14.7 %reduce-scatter.35.cloned.1.call-done = f32[64,1024]{1,0:T(8,128)} async-done(((f32[256,1024]{1,0:T(8,128)}), f32[64,1024]{1,0:T(8,128)}) %reduce-scatter.35.cloned.1.call-update) | async-done | bytes 262160 | tf_op jit(solution)/shard_map/reduce_scatter | solution.py:211
  842.5 26.7 %reduce-scatter.27.cloned.1.call-done = f32[64,1024]{1,0:T(8,128)} async-done(((f32[256,1024]{1,0:T(8,128)}), f32[64,1024]{1,0:T(8,128)}) %reduce-scatter.27.cloned.1.call-update) | async-done | bytes 262160 | tf_op jit(solution)/shard_map/reduce_scatter | solution.py:211
  870.2 26.4 %reduce-scatter.19.cloned.1.call-done = f32[64,1024]{1,0:T(8,128)} async-done(((f32[256,1024]{1,0:T(8,128)}), f32[64,1024]{1,0:T(8,128)}) %reduce-scatter.19.cloned.1.call-update) | async-done | bytes 262160 | tf_op jit(solution)/shard_map/reduce_scatter | solution.py:211
  (221 shorter events, 80.7 us)
Async XLA Ops:
  6.5 48.9 %copy-start = (bf16[1024,256]{1,0:T(8,128)(2,1)S(1)}, bf16[1024,256]{1,0:T(8,128)(2,1)}, u32[]{:S(2)}) copy-start(bf16[1024,256]{1,0:T(8,128)(2,1)} %param.29) | copy-start | bytes 1572868
  6.5 25.7 %copy-start.9 = (bf16[1024]{0:T(1024)(128)(2,1)S(1)}, bf16[1024]{0:T(1024)(128)(2,1)}, u32[]{:S(2)}) copy-start(bf16[1024]{0:T(1024)(128)(2,1)} %param.27) | copy-start | bytes 6148
  6.5 217.7 %reduce-scatter.15.cloned.1.call-start = ((), (), s32[]{:S(2)}) async-start(), calls=%async_computation.25 | async-start | bytes 294912 | tf_op jit(solution)/shard_map/reduce_scatter | solution.py:150
  31.1 0.8 copy-start.3
  55.4 7.5 copy-start.4
  56.4 172.5 %reduce-scatter.23.cloned.1.call-start = ((), (), s32[]{:S(2)}) async-start(), calls=%async_computation.29 | async-start | bytes 294912 | tf_op jit(solution)/shard_map/reduce_scatter | solution.py:150
  57.5 185.0 %reduce-scatter.17.cloned.1.call-start = ((), (), s32[]{:S(2)}) async-start(), calls=%async_computation.26 | async-start | bytes 294912 | tf_op jit(solution)/shard_map/reduce_scatter | solution.py:151
  59.7 246.4 %reduce-scatter.25.cloned.1.call-start = ((), (), s32[]{:S(2)}) async-start(), calls=%async_computation.30 | async-start | bytes 294912 | tf_op jit(solution)/shard_map/reduce_scatter | solution.py:151
  61.8 307.8 %reduce-scatter.31.cloned.1.call-start = ((), (), s32[]{:S(2)}) async-start(), calls=%async_computation.33 | async-start | bytes 294912 | tf_op jit(solution)/shard_map/reduce_scatter | solution.py:150
  62.9 370.2 %reduce-scatter.33.cloned.1.call-start = ((), (), s32[]{:S(2)}) async-start(), calls=%async_computation.34 | async-start | bytes 294912 | tf_op jit(solution)/shard_map/reduce_scatter | solution.py:151
  64.0 439.6 %reduce-scatter.21.cloned.1.call-start = ((), (), s32[]{:S(2)}) async-start(), calls=%async_computation.28 | async-start | bytes 2359296 | tf_op jit(solution)/shard_map/reduce_scatter | solution.py:149
  91.7 16.6 %copy-start.8 = (s32[2]{0:T(128)S(1)}, s32[2]{0:T(128)}, u32[]{:S(2)}) copy-start(s32[2]{0:T(128)} %param.36) | copy-start | bytes 28
  164.7 409.1 %reduce-scatter.29.cloned.1.call-start = ((), (), s32[]{:S(2)}) async-start(), calls=%async_computation.32 | async-start | bytes 2359296 | tf_op jit(solution)/shard_map/reduce_scatter | solution.py:149
  170.2 473.8 %reduce-scatter.13.cloned.1.call-start = ((), (), s32[]{:S(2)}) async-start(), calls=%async_computation.24 | async-start | bytes 2359296 | tf_op jit(solution)/shard_map/reduce_scatter | solution.py:149
  170.7 4.9 copy-start.10
  225.6 208.9 %all-to-all-start.1 = ((bf16[4,8,256]{2,1,0:T(8,128)(2,1)}), bf16[4,8,256]{2,1,0:T(8,128)(2,1)S(1)}, u32[]{:S(2)}, u32[]{:S(2)}) async-start(bf16[4,8,256]{2,1,0:T(8,128)(2,1)} %convert_bitcast_fusion.15), calls=%async_computation.3 | async-start | bytes 32768 | tf_op jit(solution)/shard_map/all_to_all | solution.py:157
  434.5 7.1 all-to-all-start.5
  441.6 7.1 all-to-all-start.9
  448.6 7.5 all-to-all-start.2
  456.1 7.1 all-to-all-start.6
  505.2 140.4 %all-to-all-start.4 = ((bf16[4,8,2048]{2,1,0:T(8,128)(2,1)}), bf16[4,8,2048]{2,1,0:T(8,128)(2,1)S(1)}, u32[]{:S(2)}, u32[]{:S(2)}) async-start(bf16[4,8,2048]{2,1,0:T(8,128)(2,1)} %convert_bitcast_fusion.6), calls=%async_computation.9 | async-start | bytes 262144 | tf_op jit(solution)/shard_map/all_to_all | solution.py:154
  645.6 7.9 all-to-all-start.8
  653.5 9.9 %all-to-all-start.10 = ((bf16[4,8,256]{2,1,0:T(8,128)(2,1)}), bf16[4,8,256]{2,1,0:T(8,128)(2,1)S(1)}, u32[]{:S(2)}, u32[]{:S(2)}) async-start(bf16[4,8,256]{2,1,0:T(8,128)(2,1)} %convert_bitcast_fusion.10), calls=%async_computation.21 | async-start | bytes 32768 | tf_op jit(solution)/shard_map/all_to_all | solution.py:160
  657.1 4.3 copy-start.2
  663.4 7.9 all-to-all-start
  671.7 4.8 copy-start.11
  678.0 7.9 all-to-all-start.11
  685.9 7.9 all-to-all-start.7
  693.9 11.4 %all-to-all-start.3 = ((bf16[8,4,2048]{2,0,1:T(8,128)(2,1)}), bf16[8,4,2048]{2,0,1:T(8,128)(2,1)S(1)}, u32[]{:S(2)}, u32[]{:S(2)}) async-start(bf16[8,4,2048]{2,0,1:T(8,128)(2,1)} %copy.82), calls=%async_computation.6 | async-start | bytes 262144 | tf_op jit(solution)/shard_map/all_to_all | solution.py:184
  697.2 144.4 %reduce-scatter.35.cloned.1.call-start = ((), (), s32[]{:S(2)}) async-start(), calls=%async_computation.35 | async-start | bytes 1310720 | tf_op jit(solution)/shard_map/reduce_scatter | solution.py:211
  702.8 9.2 %collective-permute-start.14 = (bf16[32,2048]{1,0:T(8,128)(2,1)S(1)}, bf16[32,2048]{1,0:T(8,128)(2,1)S(1)}, u32[]{:S(2)}, u32[]{:S(2)}) collective-permute-start(bf16[32,2048]{1,0:T(8,128)(2,1)S(1)} %bitcast.305), channel_id=1, source_target_pairs={{0,4},{4,8},{8,12},{12,16},{16,20},{20,24},{24,28},{28,0},{1,5},{5... | collective-permute-start | bytes 393224 | tf_op jit(solution)/shard_map/ppermute | solution.py:195
  703.7 11.1 %collective-permute-start.7 = (bf16[32,2048]{1,0:T(8,128)(2,1)S(1)}, bf16[32,2048]{1,0:T(8,128)(2,1)S(1)}, u32[]{:S(2)}, u32[]{:S(2)}) collective-permute-start(bf16[32,2048]{1,0:T(8,128)(2,1)S(1)} %bitcast.306), channel_id=1, source_target_pairs={{0,4},{4,8},{8,12},{12,16},{16,20},{20,24},{24,28},{28,0},{1,5},{5... | collective-permute-start | bytes 393224 | tf_op jit(solution)/shard_map/ppermute | solution.py:195
  705.3 12.3 %collective-permute-start = (bf16[32,2048]{1,0:T(8,128)(2,1)S(1)}, bf16[32,2048]{1,0:T(8,128)(2,1)S(1)}, u32[]{:S(2)}, u32[]{:S(2)}) collective-permute-start(bf16[32,2048]{1,0:T(8,128)(2,1)S(1)} %bitcast.307), channel_id=1, source_target_pairs={{0,4},{4,8},{8,12},{12,16},{16,20},{20,24},{24,28},{28,0},{1,5},{5... | collective-permute-start | bytes 393224 | tf_op jit(solution)/shard_map/ppermute | solution.py:195
  712.0 8.6 collective-permute-start.15
  714.8 8.6 collective-permute-start.8
  717.6 9.1 %collective-permute-start.1 = (bf16[32,2048]{1,0:T(8,128)(2,1)S(1)}, bf16[32,2048]{1,0:T(8,128)(2,1)S(1)}, u32[]{:S(2)}, u32[]{:S(2)}) collective-permute-start(bf16[32,2048]{1,0:T(8,128)(2,1)S(1)} %collective-permute-done), channel_id=1, source_target_pairs={{0,4},{4,8},{8,12},{12,16},{16,20},{20,24},{24,28},{28,0},{1,5},{5... | collective-permute-start | bytes 393224 | tf_op jit(solution)/shard_map/ppermute | solution.py:195
  720.6 9.1 %collective-permute-start.16 = (bf16[32,2048]{1,0:T(8,128)(2,1)S(1)}, bf16[32,2048]{1,0:T(8,128)(2,1)S(1)}, u32[]{:S(2)}, u32[]{:S(2)}) collective-permute-start(bf16[32,2048]{1,0:T(8,128)(2,1)S(1)} %collective-permute-done.15), channel_id=1, source_target_pairs={{0,4},{4,8},{8,12},{12,16},{16,20},{20,24},{24,28},{28,0},{1,5},{5... | collective-permute-start | bytes 393224 | tf_op jit(solution)/shard_map/ppermute | solution.py:195
  723.4 9.1 %collective-permute-start.9 = (bf16[32,2048]{1,0:T(8,128)(2,1)S(1)}, bf16[32,2048]{1,0:T(8,128)(2,1)S(1)}, u32[]{:S(2)}, u32[]{:S(2)}) collective-permute-start(bf16[32,2048]{1,0:T(8,128)(2,1)S(1)} %collective-permute-done.8), channel_id=1, source_target_pairs={{0,4},{4,8},{8,12},{12,16},{16,20},{20,24},{24,28},{28,0},{1,5},{5... | collective-permute-start | bytes 393224 | tf_op jit(solution)/shard_map/ppermute | solution.py:195
  726.7 8.8 collective-permute-start.2
  729.8 8.7 collective-permute-start.17
  732.5 9.0 collective-permute-start.10
  735.5 9.1 %collective-permute-start.3 = (bf16[32,2048]{1,0:T(8,128)(2,1)S(1)}, bf16[32,2048]{1,0:T(8,128)(2,1)S(1)}, u32[]{:S(2)}, u32[]{:S(2)}) collective-permute-start(bf16[32,2048]{1,0:T(8,128)(2,1)S(1)} %collective-permute-done.2), channel_id=1, source_target_pairs={{0,4},{4,8},{8,12},{12,16},{16,20},{20,24},{24,28},{28,0},{1,5},{5... | collective-permute-start | bytes 393224 | tf_op jit(solution)/shard_map/ppermute | solution.py:195
  738.4 8.9 collective-permute-start.18
  741.5 9.0 collective-permute-start.11
  744.6 8.8 collective-permute-start.4
  747.4 9.1 %collective-permute-start.19 = (bf16[32,2048]{1,0:T(8,128)(2,1)S(1)}, bf16[32,2048]{1,0:T(8,128)(2,1)S(1)}, u32[]{:S(2)}, u32[]{:S(2)}) collective-permute-start(bf16[32,2048]{1,0:T(8,128)(2,1)S(1)} %collective-permute-done.18), channel_id=1, source_target_pairs={{0,4},{4,8},{8,12},{12,16},{16,20},{20,24},{24,28},{28,0},{1,5},{5... | collective-permute-start | bytes 393224 | tf_op jit(solution)/shard_map/ppermute | solution.py:195
  750.6 9.1 %collective-permute-start.12 = (bf16[32,2048]{1,0:T(8,128)(2,1)S(1)}, bf16[32,2048]{1,0:T(8,128)(2,1)S(1)}, u32[]{:S(2)}, u32[]{:S(2)}) collective-permute-start(bf16[32,2048]{1,0:T(8,128)(2,1)S(1)} %collective-permute-done.11), channel_id=1, source_target_pairs={{0,4},{4,8},{8,12},{12,16},{16,20},{20,24},{24,28},{28,0},{1,5},{5... | collective-permute-start | bytes 393224 | tf_op jit(solution)/shard_map/ppermute | solution.py:195
  753.4 8.8 collective-permute-start.5
  756.5 8.4 collective-permute-start.20
  759.7 7.7 collective-permute-start.13
  762.3 7.7 collective-permute-start.6
  764.9 5.0 copy-start.5
  767.4 2.6 copy-start.6
  812.0 5.3 copy-start.7
  816.9 52.3 %reduce-scatter.27.cloned.1.call-start = ((), (), s32[]{:S(2)}) async-start(), calls=%async_computation.31 | async-start | bytes 1310720 | tf_op jit(solution)/shard_map/reduce_scatter | solution.py:211
  821.8 74.8 %reduce-scatter.19.cloned.1.call-start = ((), (), s32[]{:S(2)}) async-start(), calls=%async_computation.27 | async-start | bytes 1310720 | tf_op jit(solution)/shard_map/reduce_scatter | solution.py:211
  822.2 76.1 %copy-start.1 = (bf16[1024,256]{1,0:T(8,128)(2,1)S(1)}, bf16[1024,256]{1,0:T(8,128)(2,1)}, u32[]{:S(2)}) copy-start(bf16[1024,256]{1,0:T(8,128)(2,1)} %param.29) | copy-start | bytes 1572868
Sparse Core Ops, SparseCore 0:
  56.6 58.5 reduce-scatter.14
  118.5 60.3 reduce-scatter.22
  182.2 60.3 reduce-scatter.16
  245.7 60.3 reduce-scatter.24
  309.3 60.2 reduce-scatter.30
  372.8 60.2 reduce-scatter.32
  436.7 66.8 reduce-scatter.20
  507.1 66.6 reduce-scatter.28
  577.3 66.6 reduce-scatter.12
  817.0 24.4 reduce-scatter.34
  844.3 24.8 reduce-scatter.26
  871.6 24.9 reduce-scatter.18
